TPU v7x, 512 devices: a whole 4x8x8 slice. The times are simulated.
512 devices in a mesh: row: 16 (over z, core), col: 32 (over x, y).
Axes of the slice: x: 4, y: 8, z: 8, core: 2. Of those that a mesh axis runs over, the one named last changes fastest.
Arguments:
- pool: float32 [131072, 256], P(('row', 'col')), may hold values from -12 to 12
- row_pick: int32 [65536], replicated, may hold values from 0 to 8191, as said below
- length_scale: float32 [256], replicated, may hold values from 12 to 48
- panel_tile: int32 [1], replicated, may hold values from 0 to 959
Outputs:
- schur: float32 [65536, 4096], P('row', 'col')
- row_panel: float32 [65536, 64], P('row')
Inputs may be any that keep to these rules, and one draw needn't show every extreme that they name: `row_pick`: entry m indexes the 8192 pixels of tile-grid row m // 4096; entries of one tile-grid row are distinct, at most 160 of them lie in the 256 pixels of one device, and exactly 160 do for some device of each tile-grid row.
All inputs are finite; a program needn't handle non-finite values.
Results may differ from a plain program's by a relative error of at most 0.0003.
Values sent between devices are 32-bit elements; how exact they have to be, the bound alone decides.
No kernel may reach another device: no remote copies, remote signals or barrier semaphores. Data moves between devices by JAX's collectives and lax.ppermute only.
A program may use at most 64 MiB of HBM per device.

v0:
```python
import jax
import jax.numpy as jnp
from jax import lax
from jax.sharding import PartitionSpec as P

TB = 64
WT = 2
noise_level = 0.1
root_five = 5.0**0.5


def from_root(x, axis, root):
    mine = lax.axis_index(axis) == root
    return lax.psum(jnp.where(mine, x, jnp.zeros_like(x)), axis)


def kernel(left, right, left_index, right_index):
    left_sq = jnp.sum(left * left, axis=1)
    right_sq = jnp.sum(right * right, axis=1)
    cross = jnp.dot(
        left, right.T, precision=lax.Precision.HIGHEST, preferred_element_type=jnp.float32
    )
    dist_sq = jnp.maximum(left_sq[:, None] + right_sq[None, :] - 2.0 * cross, 0.0)
    radius = jnp.sqrt(dist_sq)
    value = (1.0 + root_five * radius + 5.0 / 3.0 * dist_sq) * jnp.exp(-root_five * radius)
    same = (left_index[:, None] == right_index[None, :]).astype(value.dtype)
    return value + noise_level * same


def panel_solve(factor, block):
    return lax.linalg.triangular_solve(factor, block, left_side=False, lower=True, transpose_a=True)


def body(pool, row_pick, length_scale, panel_tile):
    rows_count = lax.axis_size("row")
    cols_count = lax.axis_size("col")
    my_row = lax.axis_index("row")
    my_col = lax.axis_index("col")
    total_rows = row_pick.shape[0]
    local_rows = total_rows // rows_count
    my_pick = lax.dynamic_slice_in_dim(row_pick, my_row * local_rows, local_rows)
    gathered = lax.all_gather(pool, "col", axis=0, tiled=True)
    features = jnp.take(gathered, my_pick, axis=0)
    panel = panel_tile[0]
    tiles = panel + 1 + jnp.mod(my_col - panel - 1, cols_count) + cols_count * jnp.arange(WT)
    local_tiles = tiles // rows_count
    col_source = (local_tiles[:, None] * TB + jnp.arange(TB)[None, :]).reshape(-1)
    col_local = jnp.take(features, col_source, axis=0)
    col_feats = from_root(col_local, "row", my_col % rows_count)
    panel_row = panel % rows_count
    panel_local = panel // rows_count
    panel_rows = lax.dynamic_slice_in_dim(features, panel_local * TB, TB)
    panel_feats = from_root(panel_rows, "row", panel_row)
    inverse_scale = 1.0 / length_scale
    scaled_rows = features * inverse_scale
    scaled_cols = col_feats * inverse_scale
    scaled_panel = panel_feats * inverse_scale
    local_index = jnp.arange(local_rows)
    row_global = (local_index // TB * rows_count + my_row) * TB + local_index % TB
    col_global = (tiles[:, None] * TB + jnp.arange(TB)[None, :]).reshape(-1)
    panel_global = panel * TB + jnp.arange(TB)
    factor = jnp.linalg.cholesky(kernel(scaled_panel, scaled_panel, panel_global, panel_global))
    row_panel = panel_solve(factor, kernel(scaled_rows, scaled_panel, row_global, panel_global))
    col_panel = panel_solve(factor, kernel(scaled_cols, scaled_panel, col_global, panel_global))
    update = jnp.dot(
        row_panel, col_panel.T, precision=lax.Precision.HIGHEST, preferred_element_type=jnp.float32
    )
    schur = kernel(scaled_rows, scaled_cols, row_global, col_global) - update
    return (schur, row_panel)


def solution(mesh):
    in_specs = (P(("row", "col"), None), P(), P(), P())
    out_specs = (P("row", "col"), P("row", None))
    return jax.shard_map(body, mesh=mesh, in_specs=in_specs, out_specs=out_specs, check_vma=False)
```

profile of v0, /device:TPU:1, one launch (start us, length us, event | category | flops | bytes accessed | tf_op | source)
XLA Modules:
  0.0 298.0 jit_solution(12258355929983849131)
XLA Ops:
  7.2 0.7 all-gather.2.cloned.1.call-update
  9.1 0.7 compare_and_fusion
  9.8 0.7 fusion.75
  10.5 0.7 broadcast_divide_fusion
  11.2 107.6 %all-gather.2.cloned.1.call-done = f32[8192,256]{1,0:T(8,128)} async-done(((f32[256,256]{1,0:T(8,128)}), f32[8192,256]{1,0:T(8,128)}) %all-gather.2.cloned.1.call-update) | async-done | bytes 8388624 | tf_op jit(solution)/shard_map/all_gather | solution.py:42
  118.9 19.5 %gather_fusion = f32[4096,256]{1,0:T(8,128)} fusion(f32[8192,256]{1,0:T(8,128)} %all-gather.2.cloned.1.call-done, s32[4096]{0:T(1024)S(1)} %fusion.75), kind=kCustom, calls=%fused_computation | custom fusion | bytes 8404992 | tf_op jit(solution)/shard_map/jit(_take)/gather | solution.py:43
  138.3 4.1 %multiply_reduce_fusion = (f32[4096]{0:T(1024)S(1)}, f32[4096,256]{1,0:T(8,128)}) fusion(f32[256]{0:T(256)S(1)} %broadcast_divide_fusion, f32[4096,256]{1,0:T(8,128)} %gather_fusion, pred[4096]{0:T(1024)(128)(4,1)S(1)} %compare_and_fusion), kind=kLoop, calls=%fused_computation.9 | loop fusion | flops 4190208 | bytes 8410112 | tf_op jit(solution)/shard_map/reduce_sum | solution.py:18
  142.4 2.9 gather_fusion.1
  145.4 1.5 dynamic-slice_select_fusion
  146.8 0.7 select_select_fusion
  147.6 110.7 %all-reduce.3.cloned.1.call-done = (f32[64,256]{1,0:T(8,128)}, f32[128,256]{1,0:T(8,128)}) async-done(((f32[64,256]{1,0:T(8,128)}, f32[128,256]{1,0:T(8,128)}), (f32[64,256]{1,0:T(8,128)}, f32[128,256]{1,0:T(8,128)})) %all-reduce.3.cloned.1.call-update) | async-done | bytes 196624 | tf_op jit(solution)/shard_map/psum | solution.py:14
  258.3 0.9 multiply_reduce_fusion.2
  259.3 1.1 fusion.91
  260.5 6.6 %fusion.3 = f32[4096,64]{0,1:T(8,128)S(1)} fusion(f32[4096,256]{1,0:T(8,128)} %get-tuple-element.7, f32[256]{0:T(256)S(1)} %broadcast_divide_fusion, f32[64]{0:T(128)S(1)} %multiply_reduce_fusion.2, f32[4096]{0:T(1024)S(1)} %get-tuple-element.6, f32[64,256]{1,0:T(8,128)} %get-tuple-element.2), kind=kOutput, calls=%fused_computation.8 | convolution fusion | flops 807419904 | bytes 5326080 | tf_op jit(solution)/shard_map/dot_general | solution.py:20
  267.1 0.1 multiply_reduce_fusion.1
  267.2 0.3 fusion.9
  267.5 3.4 %fusion.1 = f32[4096,128]{1,0:T(8,128)S(1)} fusion(f32[4096,256]{1,0:T(8,128)S(1)} %copy-done, f32[256]{0:T(256)S(1)} %broadcast_divide_fusion, f32[128]{0:T(128)S(1)} %multiply_reduce_fusion.1, f32[4096]{0:T(1024)S(1)} %get-tuple-element.6, f32[128,256]{1,0:T(8,128)S(1)} %copy-done.1), kind=kOutput, calls=%fused_computation.5 | convolution fusion | flops 1613791232 | bytes 6440448 | tf_op jit(solution)/shard_map/dot_general | solution.py:20
  271.3 5.8 %cholesky.15 = f32[64,64]{1,0:T(8,128)S(1)} custom-call(f32[64,64]{1,0:T(8,128)S(1)} %add_multiply_fusion), custom_call_target="Cholesky" | custom-call | tf_op jit(solution)/shard_map/jit(cholesky)/cholesky | solution.py:62
  277.2 0.6 compare_reduce_fusion
  277.8 0.7 fusion.37
  278.5 4.9 %custom-call.8 = f32[1,64,64]{1,2,0:T(8,128)S(1)} custom-call(f32[1,64,64]{2,1,0:T(8,128)S(1)} %fusion.37), custom_call_target="InvertDiagBlocksLowerTriangular" | custom-call | tf_op jit(solution)/shard_map/triangular_solve | solution.py:31
  283.4 1.7 fusion.10
  285.1 0.4 fusion.38
  285.5 5.7 %convolution_subtract_fusion = f32[4096,128]{1,0:T(8,128)} fusion(f32[4096,64]{0,1:T(8,128)S(1)} %fusion.10, f32[128,64]{1,0:T(8,128)S(1)} %fusion.38, f32[4096,128]{1,0:T(8,128)S(1)} %fusion.1, s32[128]{0:T(128)S(1)} %add.328, s32[4096]{0:T(1024)S(1)} %fusion.65), kind=kOutput, calls=%fused_computation.2 | convolution fusion | flops 407896064 | bytes 5292544 | tf_op jit(solution)/shard_map/dot_general | solution.py:65
  (27 shorter events, 0.9 us)
Async XLA Ops:
  7.2 111.7 %all-gather.2.cloned.1.call-start = ((), (), s32[]{:S(2)}) async-start(), calls=%async_computation | async-start | bytes 8650752 | tf_op jit(solution)/shard_map/all_gather | solution.py:42
  7.9 250.4 %all-reduce.3.cloned.1.call-start = ((), (), s32[]{:S(2)}) async-start(), calls=%async_computation.1 | async-start | bytes 393216 | tf_op jit(solution)/shard_map/psum | solution.py:14
  260.4 6.7 %copy-start.1 = (f32[128,256]{1,0:T(8,128)S(1)}, f32[128,256]{1,0:T(8,128)}, u32[]{:S(2)}) copy-start(f32[128,256]{1,0:T(8,128)} %get-tuple-element.3) | copy-start | bytes 393220
  260.4 6.8 %copy-start.2 = (f32[64,256]{1,0:T(8,128)S(1)}, f32[64,256]{1,0:T(8,128)}, u32[]{:S(2)}) copy-start(f32[64,256]{1,0:T(8,128)} %get-tuple-element.2) | copy-start | bytes 196612
  260.5 7.0 %copy-start = (f32[4096,256]{1,0:T(8,128)S(1)}, f32[4096,256]{1,0:T(8,128)}, u32[]{:S(2)}) copy-start(f32[4096,256]{1,0:T(8,128)} %get-tuple-element.7) | copy-start | bytes 12582916
  285.1 6.0 %copy-start.3 = (f32[4096,64]{0,1:T(8,128)}, f32[4096,64]{0,1:T(8,128)S(1)}, u32[]{:S(2)}) copy-start(f32[4096,64]{0,1:T(8,128)S(1)} %fusion.10) | copy-start | bytes 3145732
Sparse Core Ops, SparseCore 0:
  11.1 107.6 all-gather.1
  147.7 110.5 all-reduce.2
where the time goes:
time: 298 us
  waiting for transfers between devices  219 us (73%)
  local copies, waits for them, and re-layouts  22.9 us (8%)
  other arithmetic  21.9 us (7%)
  matrix products  19.2 us (6%)
  between operations  14.9 us (5%)
    psum x1, waiting for transfers between devices, from_root(): return lax.psum(jnp.where(mine, x, jnp.zeros_like(x)), axis)  111 us
    all_gather x1, waiting for transfers between devices, body(): gathered = lax.all_gather(pool, 'col', axis=0, tiled=True)  108 us
    gather x1, local copies, waits for them, and re-layouts, body(): features = jnp.take(gathered, my_pick, axis=0)  19.5 us
    dot_general x4, matrix products, kernel(): jnp.dot(left, right.T, precision=lax.Precision.HIGHEST, preferred_element...  11.5 us
    another operation x3, other arithmetic, body(): jnp.linalg.cholesky(kernel(scaled_panel, scaled_panel, panel_global, pane...  6.52 us
  transfers between devices with their start and end apart: 2, of which 2 were waited for; matrix products, arithmetic and copies ran while one was open for 1% of the time, Pallas kernels for 0%

commit v1 on v0

--- a/solution.py
+++ b/solution.py
@@ -39,7 +39,9 @@
     total_rows = row_pick.shape[0]
     local_rows = total_rows // rows_count
     my_pick = lax.dynamic_slice_in_dim(row_pick, my_row * local_rows, local_rows)
-    gathered = lax.all_gather(pool, "col", axis=0, tiled=True)
+    gathered = jnp.concatenate(
+        lax.all_to_all(jnp.stack([pool] * lax.axis_size("col"), axis=0), "col", 0, 0), 0
+    )
     features = jnp.take(gathered, my_pick, axis=0)
     panel = panel_tile[0]
     tiles = panel + 1 + jnp.mod(my_col - panel - 1, cols_count) + cols_count * jnp.arange(WT)

time: 298 us -> 398 us (1.34)
  waiting for transfers between devices: 219 us -> 304 us
  starting transfers between devices: 0.08 us -> 10.8 us
  local copies, waits for them, and re-layouts: 22.9 us -> 28 us
    all_to_all x0 -> x1, waiting for transfers between devices: none -> 181 us  [body(): lax.all_to_all(jnp.stack([pool] * lax.axis_size('col'), axis=0), 'col', 0...]
    all_gather x1 -> x0, waiting for transfers between devices: 108 us -> none  [body(): gathered = lax.all_gather(pool, 'col', axis=0, tiled=True)]
    psum x1, waiting for transfers between devices: 111 us -> 123 us  [from_root(): return lax.psum(jnp.where(mine, x, jnp.zeros_like(x)), axis)]
    all_to_all x0 -> x1, starting transfers between devices: none -> 10.7 us  [body(): lax.all_to_all(jnp.stack([pool] * lax.axis_size('col'), axis=0), 'col', 0...]
    another operation x0 -> x1, local copies, waits for them, and re-layouts: none -> 5.11 us  [body(): jnp.stack([pool] * lax.axis_size('col'), axis=0)]
  transfers between devices with their start and end apart: 2 -> 2, of which waited for: 2 -> 2; matrix products, arithmetic and copies ran while one was open for 1% -> 0% of each run, Pallas kernels for 0% -> 0%
where the time goes in v1:
time: 398 us
  waiting for transfers between devices  304 us (76%)
  local copies, waits for them, and re-layouts  28 us (7%)
  other arithmetic  21.2 us (5%)
  matrix products  19.2 us (5%)
  between operations  14.9 us (4%)
  starting transfers between devices  10.8 us (3%)
    all_to_all x1, waiting for transfers between devices, body(): lax.all_to_all(jnp.stack([pool] * lax.axis_size('col'), axis=0), 'col', 0...  181 us
    psum x1, waiting for transfers between devices, from_root(): return lax.psum(jnp.where(mine, x, jnp.zeros_like(x)), axis)  123 us
    gather x1, local copies, waits for them, and re-layouts, body(): features = jnp.take(gathered, my_pick, axis=0)  19.5 us
    dot_general x4, matrix products, kernel(): jnp.dot(left, right.T, precision=lax.Precision.HIGHEST, preferred_element...  11.5 us
    all_to_all x1, starting transfers between devices, body(): lax.all_to_all(jnp.stack([pool] * lax.axis_size('col'), axis=0), 'col', 0...  10.7 us
  transfers between devices with their start and end apart: 2, of which 2 were waited for; matrix products, arithmetic and copies ran while one was open for 0% of the time, Pallas kernels for 0%

profile of v1, /device:TPU:1, one launch (start us, length us, event | category | flops | bytes accessed | tf_op | source)
XLA Modules:
  0.0 397.9 jit_solution(2808629964894247682)
XLA Ops:
  7.2 5.1 %stack.2 = f32[32,256,256]{2,1,0:T(8,128)} broadcast(f32[256,256]{1,0:T(8,128)} %param.4), dimensions={1,2} | broadcast | bytes 8650752 | tf_op jit(solution)/shard_map/stack | solution.py:43
  12.3 10.7 %all-to-all-start = ((f32[32,256,256]{2,1,0:T(8,128)}), f32[32,256,256]{2,1,0:T(8,128)}, u32[]{:S(2)}, u32[]{:S(2)}) async-start(f32[32,256,256]{2,1,0:T(8,128)} %stack.2), calls=%async_computation | async-start | bytes 16777216 | tf_op jit(solution)/shard_map/all_to_all | solution.py:43
  24.2 0.7 compare_and_fusion
  24.9 0.7 fusion.75
  25.7 181.0 %all-to-all-done = f32[32,256,256]{2,1,0:T(8,128)} async-done(((f32[32,256,256]{2,1,0:T(8,128)}), f32[32,256,256]{2,1,0:T(8,128)}, u32[]{:S(2)}, u32[]{:S(2)}) %all-to-all-start) | async-done | bytes 8388640 | tf_op jit(solution)/shard_map/all_to_all | solution.py:43
  206.7 19.5 %gather_fusion = f32[4096,256]{1,0:T(8,128)} fusion(f32[8192,256]{1,0:T(8,128)} %bitcast, s32[4096]{0:T(1024)S(1)} %fusion.75), kind=kCustom, calls=%fused_computation | custom fusion | bytes 8404992 | tf_op jit(solution)/shard_map/jit(_take)/gather | solution.py:45
  226.1 4.1 %multiply_reduce_fusion = (f32[4096]{0:T(1024)S(1)}, f32[4096,256]{1,0:T(8,128)}) fusion(f32[256]{0:T(256)S(1)} %broadcast_divide_fusion, f32[4096,256]{1,0:T(8,128)} %gather_fusion, pred[4096]{0:T(1024)(128)(4,1)S(1)} %compare_and_fusion), kind=kLoop, calls=%fused_computation.9 | loop fusion | flops 4190208 | bytes 8410112 | tf_op jit(solution)/shard_map/reduce_sum | solution.py:18
  230.2 2.9 gather_fusion.1
  233.2 1.5 dynamic-slice_select_fusion
  234.7 0.7 select_select_fusion
  235.5 122.8 %all-reduce.3.cloned.1.call-done = (f32[64,256]{1,0:T(8,128)}, f32[128,256]{1,0:T(8,128)}) async-done(((f32[64,256]{1,0:T(8,128)}, f32[128,256]{1,0:T(8,128)}), (f32[64,256]{1,0:T(8,128)}, f32[128,256]{1,0:T(8,128)})) %all-reduce.3.cloned.1.call-update) | async-done | bytes 196624 | tf_op jit(solution)/shard_map/psum | solution.py:14
  358.3 0.9 multiply_reduce_fusion.2
  359.2 1.1 fusion.91
  360.4 6.6 %fusion.3 = f32[4096,64]{0,1:T(8,128)S(1)} fusion(f32[4096,256]{1,0:T(8,128)} %get-tuple-element.7, f32[256]{0:T(256)S(1)} %broadcast_divide_fusion, f32[64]{0:T(128)S(1)} %multiply_reduce_fusion.2, f32[4096]{0:T(1024)S(1)} %get-tuple-element.6, f32[64,256]{1,0:T(8,128)} %get-tuple-element.2), kind=kOutput, calls=%fused_computation.8 | convolution fusion | flops 807419904 | bytes 5326080 | tf_op jit(solution)/shard_map/dot_general | solution.py:20
  367.1 0.1 multiply_reduce_fusion.1
  367.2 0.3 fusion.9
  367.5 3.4 fusion.1
  371.2 5.8 %cholesky.15 = f32[64,64]{1,0:T(8,128)S(1)} custom-call(f32[64,64]{1,0:T(8,128)S(1)} %add_multiply_fusion), custom_call_target="Cholesky" | custom-call | tf_op jit(solution)/shard_map/jit(cholesky)/cholesky | solution.py:64
  377.1 0.6 compare_reduce_fusion
  377.8 0.7 fusion.37
  378.4 4.9 %custom-call.8 = f32[1,64,64]{1,2,0:T(8,128)S(1)} custom-call(f32[1,64,64]{2,1,0:T(8,128)S(1)} %fusion.37), custom_call_target="InvertDiagBlocksLowerTriangular" | custom-call | tf_op jit(solution)/shard_map/triangular_solve | solution.py:31
  383.3 1.7 fusion.10
  385.1 0.4 fusion.38
  385.4 5.7 %convolution_subtract_fusion = f32[4096,128]{1,0:T(8,128)} fusion(f32[4096,64]{0,1:T(8,128)S(1)} %fusion.10, f32[128,64]{1,0:T(8,128)S(1)} %fusion.38, f32[4096,128]{1,0:T(8,128)S(1)} %fusion.1, s32[128]{0:T(128)S(1)} %add.328, s32[4096]{0:T(1024)S(1)} %fusion.65), kind=kOutput, calls=%fused_computation.2 | convolution fusion | flops 407896064 | bytes 5292544 | tf_op jit(solution)/shard_map/dot_general | solution.py:67
  (29 shorter events, 0.9 us)
Async XLA Ops:
  12.3 13.4 %copy-start.3 = (f32[256]{0:T(256)S(1)}, f32[256]{0:T(256)}, u32[]{:S(2)}) copy-start(f32[256]{0:T(256)} %param.6) | copy-start | bytes 3076
  12.3 194.4 %all-to-all-start = ((f32[32,256,256]{2,1,0:T(8,128)}), f32[32,256,256]{2,1,0:T(8,128)}, u32[]{:S(2)}, u32[]{:S(2)}) async-start(f32[32,256,256]{2,1,0:T(8,128)} %stack.2), calls=%async_computation | async-start | bytes 16777216 | tf_op jit(solution)/shard_map/all_to_all | solution.py:43
  23.0 335.3 %all-reduce.3.cloned.1.call-start = ((), (), s32[]{:S(2)}) async-start(), calls=%async_computation.1 | async-start | bytes 393216 | tf_op jit(solution)/shard_map/psum | solution.py:14
  360.4 6.7 %copy-start.1 = (f32[128,256]{1,0:T(8,128)S(1)}, f32[128,256]{1,0:T(8,128)}, u32[]{:S(2)}) copy-start(f32[128,256]{1,0:T(8,128)} %get-tuple-element.3) | copy-start | bytes 393220
  360.4 6.8 %copy-start.2 = (f32[64,256]{1,0:T(8,128)S(1)}, f32[64,256]{1,0:T(8,128)}, u32[]{:S(2)}) copy-start(f32[64,256]{1,0:T(8,128)} %get-tuple-element.2) | copy-start | bytes 196612
  360.4 7.0 %copy-start = (f32[4096,256]{1,0:T(8,128)S(1)}, f32[4096,256]{1,0:T(8,128)}, u32[]{:S(2)}) copy-start(f32[4096,256]{1,0:T(8,128)} %get-tuple-element.7) | copy-start | bytes 12582916
  385.0 6.0 %copy-start.4 = (f32[4096,64]{0,1:T(8,128)}, f32[4096,64]{0,1:T(8,128)S(1)}, u32[]{:S(2)}) copy-start(f32[4096,64]{0,1:T(8,128)S(1)} %fusion.10) | copy-start | bytes 3145732
Sparse Core Ops, SparseCore 0:
  235.6 122.6 all-reduce.2

commit v2 on v0

--- a/solution.py
+++ b/solution.py
@@ -11,7 +11,12 @@
 
 def from_root(x, axis, root):
     mine = lax.axis_index(axis) == root
-    return lax.psum(jnp.where(mine, x, jnp.zeros_like(x)), axis)
+
+    def advance_levels_all(v0, bus_axis):
+        val = jnp.sum(lax.all_gather(v0, bus_axis), axis=0)
+        return val
+
+    return advance_levels_all(jnp.where(mine, x, jnp.zeros_like(x)), axis)
 
 
 def kernel(left, right, left_index, right_index):

time: 298 us -> 249 us (0.84)
  waiting for transfers between devices: 219 us -> 167 us
    psum x1 -> x0, waiting for transfers between devices: 111 us -> none  [from_root(): return lax.psum(jnp.where(mine, x, jnp.zeros_like(x)), axis)]
    all_gather x0 -> x2, waiting for transfers between devices: none -> 57.9 us  [advance_levels_all(): val = jnp.sum(lax.all_gather(v0, bus_axis), axis=0)]
    reduce_sum x0 -> x2, other arithmetic: none -> 3.02 us  [advance_levels_all(): val = jnp.sum(lax.all_gather(v0, bus_axis), axis=0)]
  transfers between devices with their start and end apart: 2 -> 3, of which waited for: 2 -> 3; matrix products, arithmetic and copies ran while one was open for 1% -> 11% of each run, Pallas kernels for 0% -> 0%
where the time goes in v2:
time: 249 us; the launch traced here: 248 us
  waiting for transfers between devices  167 us (67%)
  local copies, waits for them, and re-layouts  24.8 us (10%)
  other arithmetic  22 us (9%)
  matrix products  19.9 us (8%)
  between operations  14.6 us (6%)
    all_gather x1, waiting for transfers between devices, body(): gathered = lax.all_gather(pool, 'col', axis=0, tiled=True)  108 us
    all_gather x2, waiting for transfers between devices, advance_levels_all(): val = jnp.sum(lax.all_gather(v0, bus_axis), axis=0)  57.9 us
    gather x1, local copies, waits for them, and re-layouts, body(): features = jnp.take(gathered, my_pick, axis=0)  19.5 us
    dot_general x4, matrix products, kernel(): jnp.dot(left, right.T, precision=lax.Precision.HIGHEST, preferred_element...  12.3 us
    another operation x3, other arithmetic, body(): jnp.linalg.cholesky(kernel(scaled_panel, scaled_panel, panel_global, pane...  6.52 us
    dot_general x1, matrix products, body(): jnp.dot(row_panel, col_panel.T, precision=lax.Precision.HIGHEST, preferre...  5.67 us
    another operation x2, other arithmetic, panel_solve(): lax.linalg.triangular_solve(factor, block, left_side=False, lower=True, t...  5.57 us
  transfers between devices with their start and end apart: 3, of which 3 were waited for; matrix products, arithmetic and copies ran while one was open for 11% of the time, Pallas kernels for 0%

profile of v2, /device:TPU:1, one launch (start us, length us, event | category | flops | bytes accessed | tf_op | source)
XLA Modules:
  0.0 248.1 jit_solution(2899267176634873931)
XLA Ops:
  7.2 0.7 all-gather.5.cloned.1.call-update
  8.6 0.7 compare_and_fusion
  9.4 0.7 fusion.76
  10.1 0.7 broadcast_divide_fusion
  10.8 108.1 %all-gather.5.cloned.1.call-done = f32[8192,256]{1,0:T(8,128)} async-done(((f32[256,256]{1,0:T(8,128)}), f32[8192,256]{1,0:T(8,128)}) %all-gather.5.cloned.1.call-update) | async-done | bytes 8388624 | tf_op jit(solution)/shard_map/all_gather | solution.py:47
  118.9 19.5 %gather_fusion = f32[4096,256]{1,0:T(8,128)} fusion(f32[8192,256]{1,0:T(8,128)} %all-gather.5.cloned.1.call-done, s32[4096]{0:T(1024)S(1)} %fusion.76), kind=kCustom, calls=%fused_computation | custom fusion | bytes 8404992 | tf_op jit(solution)/shard_map/jit(_take)/gather | solution.py:48
  138.3 2.9 %multiply_reduce_fusion = (f32[4096]{0:T(1024)S(1)}, f32[4096,256]{1,0:T(8,128)S(1)}) fusion(f32[256]{0:T(256)S(1)} %broadcast_divide_fusion, f32[4096,256]{1,0:T(8,128)} %gather_fusion, pred[4096]{0:T(1024)(128)(4,1)S(1)} %compare_and_fusion), kind=kLoop, calls=%fused_computation.9 | loop fusion | flops 4190208 | bytes 8410112 | tf_op jit(solution)/shard_map/reduce_sum | solution.py:23
  141.2 1.9 copy-done
  143.1 0.6 dynamic-slice_select_fusion
  144.2 2.9 %gather_fusion.1 = f32[128,256]{1,0:T(8,128)S(1)} fusion(f32[4096,256]{1,0:T(8,128)} %copy-done, s32[1024]{0:T(1024)S(1)} %pad_clamp_fusion), kind=kCustom, calls=%fused_computation.1 | custom fusion | bytes 262656 | tf_op jit(solution)/shard_map/jit(_take)/gather | solution.py:53
  147.1 0.7 fusion.30
  148.0 36.5 %all-gather.9.cloned.1.call-done = f32[1024,256]{1,0:T(8,128)} async-done(((f32[64,256]{1,0:T(8,128)}), f32[1024,256]{1,0:T(8,128)}) %all-gather.9.cloned.1.call-update) | async-done | bytes 1048592 | tf_op jit(solution)/shard_map/all_gather | solution.py:16
  184.5 1.3 reduce_sum.49
  186.5 5.8 %cholesky.15 = f32[64,64]{1,0:T(8,128)S(1)} custom-call(f32[64,64]{1,0:T(8,128)S(1)} %add_multiply_fusion), custom_call_target="Cholesky" | custom-call | tf_op jit(solution)/shard_map/jit(cholesky)/cholesky | solution.py:67
  192.4 0.6 compare_reduce_fusion
  193.0 0.7 fusion.38
  193.7 4.9 %custom-call.8 = f32[1,64,64]{1,2,0:T(8,128)S(1)} custom-call(f32[1,64,64]{2,1,0:T(8,128)S(1)} %fusion.38), custom_call_target="InvertDiagBlocksLowerTriangular" | custom-call | tf_op jit(solution)/shard_map/triangular_solve | solution.py:36
  198.6 6.5 %fusion.3 = f32[4096,64]{0,1:T(8,128)S(1)} fusion(f32[4096,256]{1,0:T(8,128)} %copy-done, f32[256]{0:T(256)S(1)} %broadcast_divide_fusion, f32[64]{0:T(128)S(1)} %multiply_reduce_fusion.2, f32[4096]{0:T(1024)S(1)} %get-tuple-element.4, f32[64,256]{1,0:T(8,128)S(1)} %reduce_sum.49), kind=kOutput, calls=%fused_computation.8 | convolution fusion | flops 807419904 | bytes 5326080 | tf_op jit(solution)/shard_map/dot_general | solution.py:25
  205.1 1.7 fusion.10
  206.8 21.4 %all-gather.7.cloned.1.call-done = f32[16,128,256]{2,1,0:T(8,128)} async-done(((f32[1,128,256]{2,1,0:T(8,128)}), f32[16,128,256]{2,1,0:T(8,128)}) %all-gather.7.cloned.1.call-update) | async-done | bytes 2097168 | tf_op jit(solution)/shard_map/all_gather | solution.py:16
  228.2 1.7 reduce_sum.44
  230.1 0.3 fusion.9
  230.3 5.3 %fusion.1 = f32[4096,128]{1,0:T(8,128)S(1)} fusion(f32[4096,256]{1,0:T(8,128)} %copy-done, f32[256]{0:T(256)S(1)} %broadcast_divide_fusion, f32[128]{0:T(128)S(1)} %multiply_reduce_fusion.1, f32[4096]{0:T(1024)S(1)} %get-tuple-element.4, f32[128,256]{1,0:T(8,128)S(1)} %reduce_sum.44), kind=kOutput, calls=%fused_computation.5 | convolution fusion | flops 1613791232 | bytes 6440448 | tf_op jit(solution)/shard_map/dot_general | solution.py:25
  235.9 5.7 %convolution_subtract_fusion = f32[4096,128]{1,0:T(8,128)} fusion(f32[4096,64]{0,1:T(8,128)S(1)} %fusion.10, f32[128,64]{0,1:T(8,128)S(1)} %fusion.39, f32[4096,128]{1,0:T(8,128)S(1)} %fusion.1, s32[128]{0:T(128)S(1)} %add.324, s32[4096]{0:T(1024)S(1)} %fusion.66), kind=kOutput, calls=%fused_computation.2 | convolution fusion | flops 407896064 | bytes 5292544 | tf_op jit(solution)/shard_map/dot_general | solution.py:70
  (28 shorter events, 1.6 us)
Async XLA Ops:
  7.2 111.7 %all-gather.5.cloned.1.call-start = ((), (), s32[]{:S(2)}) async-start(), calls=%async_computation | async-start | bytes 8650752 | tf_op jit(solution)/shard_map/all_gather | solution.py:47
  7.9 176.6 %all-gather.9.cloned.1.call-start = ((), (), s32[]{:S(2)}) async-start(), calls=%async_computation.2 | async-start | bytes 1114112 | tf_op jit(solution)/shard_map/all_gather | solution.py:16
  141.2 1.9 copy-start
  143.8 84.4 %all-gather.7.cloned.1.call-start = ((), (), s32[]{:S(2)}) async-start(), calls=%async_computation.1 | async-start | bytes 2228224 | tf_op jit(solution)/shard_map/all_gather | solution.py:16
  206.8 29.1 %copy-start.1 = (f32[4096,64]{0,1:T(8,128)}, f32[4096,64]{0,1:T(8,128)S(1)}, u32[]{:S(2)}) copy-start(f32[4096,64]{0,1:T(8,128)S(1)} %fusion.10) | copy-start | bytes 3145732
Sparse Core Ops, SparseCore 0:
  11.1 107.6 all-gather.4
  143.9 40.5 all-gather.8
  187.2 40.9 all-gather.6
